TPU v7x, 32 devices: a whole 2x2x4 slice. The times are simulated.
32 devices in a mesh: ctx: 4 (over z), fsdp: 2 (over y), rep: 4 (over x, core).
Axes of the slice: x: 2, y: 2, z: 4, core: 2. Of those that a mesh axis runs over, the one named last changes fastest.
Arguments:
- frames_in: bfloat16 [8, 512, 1024], P('rep', 'ctx', 'fsdp'), parts along dimension 0, may hold values from -6 to 6
- lengths: int32 [8], P('rep'), parts along dimension 0, may hold values from 128 to 512, as said below
- conv_weight: bfloat16 [16, 128, 64, 64], P('fsdp'), may hold values from -0.0625 to 0.0625
- conv_bias: bfloat16 [1024], P('fsdp'), may hold values from -3 to 3
- norm_gain: float32 [1024], replicated, may hold values from 0.1 to 1.9
- norm_shift: float32 [1024], replicated, may hold values from -3 to 3
- w_query: bfloat16 [1024, 512], replicated
- w_key: bfloat16 [1024, 512], replicated
- w_value: bfloat16 [1024, 512], replicated, may hold values from -0.1875 to 0.1875
Outputs:
- hidden: bfloat16 [8, 512, 1024], P('rep', 'ctx', 'fsdp'), parts along dimension 0
- context: bfloat16 [8, 512, 512], P(('rep', 'fsdp'), 'ctx'), parts along dimension 0
There are 4 independent parts, one for each index of `rep`. A program takes and returns all parts, laid end to end along the dimension named above; an argument that names none is the same for every part. Nothing has to cross between parts.
Inputs may be any that keep to these rules, and one draw needn't show every extreme that they name: `lengths`: one recording in every draw has all 512 frames live.
All inputs are finite; a program needn't handle non-finite values.
Results may differ from a plain program's by a relative error of at most 0.012.
Values may be sent and summed in bfloat16 or wider, within the bound.
No kernel may reach another device: no remote copies, remote signals or barrier semaphores. Data moves between devices by JAX's collectives and lax.ppermute only.
A program may use at most 128 MiB of HBM per device.

v0:
```python
import math

import jax
import jax.numpy as jnp
from jax import lax
from jax.sharding import PartitionSpec as P

HD = 64


def padded_2(x, sides, width):
    for axis, dim in sides:
        size, length = (lax.axis_size(axis), x.shape[dim])
        up = [(i, (i + 1) % size) for i in range(size - 1)]
        down = [(j, i) for i, j in up]
        last = lax.slice_in_dim(x, length - width, length, axis=dim)
        first = lax.slice_in_dim(x, 0, width, axis=dim)
        before = lax.ppermute(last, axis, up)
        after = lax.ppermute(first, axis, down)
        x = jnp.concatenate([before, x, after], axis=dim)
    return x


def attend(carry, piece, start, queries, own_length):
    best, total, accum = carry
    keys_part, vals_part = piece
    count = keys_part.shape[0]
    head_count = queries.shape[1]
    keys_part = keys_part.reshape(count, head_count, HD)
    vals_part = vals_part.reshape(count, head_count, HD)
    scores = jnp.einsum(
        "fhd,nhd->fhn", queries, keys_part, preferred_element_type=jnp.float32
    ) / math.sqrt(HD)
    valid = (start + jnp.arange(count, dtype=jnp.int32) < own_length)[None, None, :]
    scores = jnp.where(valid, scores, -1e30)
    fresh = jnp.maximum(best, jnp.max(scores, axis=2))
    weights = jnp.where(valid, jnp.exp(scores - fresh[:, :, None]), 0.0)
    factor = jnp.exp(best - fresh)
    total = total * factor + jnp.sum(weights, axis=2)
    accum = accum * factor[:, :, None] + jnp.einsum(
        "fhn,nhd->fhd", weights.astype(jnp.bfloat16), vals_part, preferred_element_type=jnp.float32
    )
    return (fresh, total, accum)


def start_state(rows, heads_here):
    return (
        jnp.full((rows, heads_here), -1e30, jnp.float32),
        jnp.zeros((rows, heads_here), jnp.float32),
        jnp.zeros((rows, heads_here, HD), jnp.float32),
    )


def blockwise(carry, all_keys, all_vals, queries, own_length, block_rows):
    block_count = all_keys.shape[0] // block_rows

    def block_step(state, index):
        begin = index * block_rows
        piece = (
            lax.dynamic_slice_in_dim(all_keys, begin, block_rows, 0),
            lax.dynamic_slice_in_dim(all_vals, begin, block_rows, 0),
        )
        return (attend(state, piece, begin, queries, own_length), None)

    final, unused = lax.scan(block_step, carry, jnp.arange(block_count, dtype=jnp.int32))
    return final


def finish(final, query_pos, own_length):
    best, total, accum = final
    result = accum / total[:, :, None]
    query_live = (query_pos < own_length)[:, None, None]
    result = jnp.where(query_live, result, 0.0)
    return result.reshape(result.shape[0], result.shape[1] * HD).astype(jnp.bfloat16)


def per_device(
    frames_in, lengths, conv_weight, conv_bias, norm_gain, norm_shift, w_query, w_key, w_value
):
    record_count, frame_rows, channels = frames_in.shape
    ctx_place = lax.axis_index("ctx")
    positions = ctx_place * frame_rows + jnp.arange(frame_rows, dtype=jnp.int32)
    live = positions[None, :] < lengths[:, None]
    masked = jnp.where(live[:, :, None], frames_in, jnp.zeros((), frames_in.dtype))
    groups_here, kernel_width, group_in, group_out = conv_weight.shape
    half_width = kernel_width // 2
    padded = padded_2(masked, (("ctx", 1),), half_width)
    kernel = conv_weight.transpose(1, 2, 0, 3).reshape(
        kernel_width, group_in, groups_here * group_out
    )
    conv_out = lax.conv_general_dilated(
        padded[:, : frame_rows + kernel_width - 1],
        kernel,
        (1,),
        "VALID",
        dimension_numbers=("NWC", "WIO", "NWC"),
        feature_group_count=groups_here,
        preferred_element_type=jnp.float32,
    )
    hidden = (
        masked.astype(jnp.float32)
        + jax.nn.gelu(conv_out + conv_bias.astype(jnp.float32), approximate=False)
    ).astype(jnp.bfloat16)
    record = lax.all_to_all(hidden, "fsdp", split_axis=0, concat_axis=2, tiled=True)
    own_length = lax.dynamic_index_in_dim(lengths, lax.axis_index("fsdp"), 0, keepdims=False)
    flat = record[0].astype(jnp.float32)
    centre = jnp.mean(flat, axis=1, keepdims=True)
    spread = jnp.mean((flat - centre) ** 2, axis=1, keepdims=True)
    normed = ((flat - centre) / jnp.sqrt(spread + 1e-05) * norm_gain + norm_shift).astype(
        jnp.bfloat16
    )
    query_flat = jnp.dot(normed, w_query, preferred_element_type=jnp.float32).astype(jnp.bfloat16)
    key_flat = jnp.dot(normed, w_key, preferred_element_type=jnp.float32).astype(jnp.bfloat16)
    val_flat = jnp.dot(normed, w_value, preferred_element_type=jnp.float32).astype(jnp.bfloat16)
    head_count = query_flat.shape[1] // HD
    queries = query_flat.reshape(frame_rows, head_count, HD)
    block_rows = 4 * frame_rows
    whole_keys, whole_vals = (
        lax.all_gather(key_flat, "ctx", axis=0, tiled=True),
        lax.all_gather(val_flat, "ctx", axis=0, tiled=True),
    )
    final = blockwise(
        start_state(frame_rows, head_count), whole_keys, whole_vals, queries, own_length, block_rows
    )
    result = finish(final, positions, own_length).reshape(1, frame_rows, head_count * HD)
    return (hidden, result)


def solution(mesh):
    in_specs = (
        P("rep", "ctx", "fsdp"),
        P("rep"),
        P("fsdp", None, None, None),
        P("fsdp"),
        P(),
        P(),
        P(),
        P(),
        P(),
    )
    out_specs = (P("rep", "ctx", "fsdp"), P(("rep", "fsdp"), "ctx", None))
    return jax.shard_map(
        per_device, mesh=mesh, in_specs=in_specs, out_specs=out_specs, check_vma=False
    )
```

profile of v0, /device:TPU:0, one launch (start us, length us, event | category | flops | bytes accessed | tf_op | source)
XLA Modules:
  0.0 133.0 jit_solution(15739627415967370258)
XLA Ops:
  0.6 0.0 copy-start
  0.7 1.2 copy.17
  1.9 0.0 copy-start.1
  1.9 0.8 broadcast_compare_fusion
  2.6 0.5 copy-done.8
  3.2 0.1 fusion.35
  3.3 4.9 %collective-permute-start = (bf16[2,64,512]{1,2,0:T(8,128)(2,1)S(1)}, bf16[2,64,512]{1,2,0:T(8,128)(2,1)S(1)}, u32[]{:S(2)}, u32[]{:S(2)}) collective-permute-start(bf16[2,64,512]{1,2,0:T(8,128)(2,1)S(1)} %get-tuple-element.22), channel_id=1, source_target_pairs={{0,8},{8,16},{16,24},{1,9},{9,17},{17,25},{2,10},{10,18},{18,26},{... | collective-permute-start | bytes 393224 | tf_op jit(solution)/shard_map/ppermute | solution.py:18
  8.3 0.0 copy-start.10
  8.3 0.0 copy-start.11
  8.3 1.3 collective-permute-start.1
  9.6 23.9 %copy.19 = bf16[8,128,64,64]{3,2,0,1:T(8,128)(2,1)} copy(bf16[8,128,64,64]{1,3,2,0:T(8,128)(2,1)} %param.11) | data formatting | bytes 16777216 | tf_op args[2]
  33.6 0.0 copy-done.1
  33.6 0.0 copy-done.10
  33.6 0.6 convert_element_type.59
  34.1 0.0 copy-done.11
  34.1 0.6 dynamic_slice.11
  34.8 0.0 collective-permute-done
  34.8 0.0 collective-permute-done.1
  34.8 0.3 pad_maximum_fusion
  35.1 2.1 %copy.18 = bf16[2,255,8,64]{3,0,2,1:T(2,128)(2,1)} copy(bf16[2,255,8,64]{1,3,2,0:T(8,128)(2,1)S(1)} %bitcast.62) | data formatting | bytes 1044480 | tf_op jit(solution)/shard_map/slice | solution.py:92
  37.2 41.1 %fusion.36 = f32[2,128,8,64]{3,0,2,1:T(2,128)S(1)} fusion(bf16[2,255,8,64]{3,0,2,1:T(2,128)(2,1)} %copy.18, bf16[8,128,64,64]{3,2,0,1:T(8,128)(2,1)} %copy.19), kind=kOutput, calls=%fused_computation.66 | convolution fusion | flops 2147483648 | bytes 9435136 | tf_op jit(solution)/shard_map/conv_general_dilated | solution.py:91
  78.3 0.0 copy-start.6
  78.3 0.0 copy-start.7
  78.3 0.7 copy.20
  79.0 0.0 copy-done.2
  79.1 2.0 %fusion.17 = bf16[2,128,512]{1,2,0:T(8,128)(2,1)} fusion(f32[2,128,8,64]{1,3,2,0:T(8,128)S(1)} %copy.20, f32[512]{0:T(512)S(1)} %copy-done.5, bf16[2,128,512]{1,2,0:T(8,128)(2,1)S(1)} %copy-done.2, pred[2,128]{1,0:T(4,128)(4,1)S(1)} %copy-done.9), kind=kLoop, calls=%fused_computation.24 | loop fusion | flops 9043968 | bytes 1050880 | tf_op jit(solution)/shard_map/convert_element_type | solution.py:103
  81.0 3.4 %all-to-all-start = ((bf16[2,128,512]{1,2,0:T(8,128)(2,1)}), bf16[2,128,512]{1,2,0:T(8,128)(2,1)S(1)}, u32[]{:S(2)}, u32[]{:S(2)}) async-start(bf16[2,128,512]{1,2,0:T(8,128)(2,1)} %fusion.17), calls=%async_computation | async-start | bytes 524288 | tf_op jit(solution)/shard_map/all_to_all | solution.py:104
  84.5 0.6 iota_compare_fusion
  85.1 0.6 broadcast_compare_fusion.1
  85.8 1.8 %copy.25 = bf16[2,128,512]{2,1,0:T(8,128)(2,1)} copy(bf16[2,128,512]{1,2,0:T(8,128)(2,1)} %fusion.17) | data formatting | bytes 524288
  87.6 2.1 %all-to-all-done = bf16[2,128,512]{1,2,0:T(8,128)(2,1)S(1)} async-done(((bf16[2,128,512]{1,2,0:T(8,128)(2,1)}), bf16[2,128,512]{1,2,0:T(8,128)(2,1)S(1)}, u32[]{:S(2)}, u32[]{:S(2)}) %all-to-all-start) | async-done | bytes 262176 | tf_op jit(solution)/shard_map/all_to_all | solution.py:104
  89.7 0.2 convert_reduce_fusion
  89.8 0.2 fusion.22
  90.0 0.3 fusion.29
  90.3 0.0 copy-done
  90.3 0.3 convolution_convert_fusion.2
  90.7 16.9 %all_gather.6 = bf16[512,512]{1,0:T(8,128)(2,1)S(1)} all-gather(bf16[128,512]{1,0:T(8,128)(2,1)S(1)} %convolution_convert_fusion.2), channel_id=1, replica_groups=mesh['ctx'=4,'fsdp'=2,'rep'=4] {'ctx'}, dimensions={0}, use_global_device_ids=true | all-gather | bytes 655360 | tf_op jit(solution)/shard_map/all_gather | solution.py:119
  107.6 1.0 copy.21
  108.6 0.3 convolution_convert_fusion.1
  108.9 0.1 copy.22
  109.1 0.0 copy-start.4
  109.1 1.8 %bitcast_reduce_fusion = (f32[128,8]{0,1:T(8,128)S(1)}, f32[8,512,128]{2,1,0:T(8,128)S(1)}) fusion(pred[512]{0:T(512)(128)(4,1)S(1)} %iota_compare_fusion, bf16[512,8,64]{0,2,1:T(8,128)(2,1)} %bitcast.63, bf16[128,8,64]{0,2,1:T(8,128)(2,1)S(1)} %bitcast.64), kind=kOutput, calls=%fused_computation.1 | convolution fusion | flops 68680704 | bytes 2757120 | tf_op jit(solution)/shard_map/while/body/eval_jaxpr/fhd,nhd->fhn/dot_general | solution.py:31
  110.9 0.6 fusion.2
  111.5 0.3 convolution_convert_fusion
  111.8 16.6 %all_gather.7 = bf16[512,512]{1,0:T(8,128)(2,1)} all-gather(bf16[128,512]{1,0:T(8,128)(2,1)S(1)} %convolution_convert_fusion), channel_id=1, replica_groups=mesh['ctx'=4,'fsdp'=2,'rep'=4] {'ctx'}, dimensions={0}, use_global_device_ids=true | all-gather | bytes 655360 | tf_op jit(solution)/shard_map/all_gather | solution.py:120
  128.5 2.0 %copy.23 = bf16[512,512]{0,1:T(8,128)(2,1)} copy(bf16[512,512]{1,0:T(8,128)(2,1)} %all_gather.7) | data formatting | bytes 1048576 | tf_op jit(solution)/shard_map/all_gather | solution.py:120
  130.5 1.8 %fusion.7 = bf16[128,8,64]{0,2,1:T(8,128)(2,1)S(1)} fusion(bf16[512,8,64]{0,2,1:T(8,128)(2,1)} %bitcast.65, f32[8,512,128]{2,1,0:T(8,128)S(1)} %get-tuple-element.35, f32[128,8]{0,1:T(8,128)S(1)} %broadcast_maximum_fusion, pred[512]{0:T(512)(128)(4,1)S(1)} %iota_compare_fusion, f32[128,8]{0,1:T(8,128)S(1)} %get-tuple-element.33, ...), kind=kOutput, calls=%fused_computation.11 | convolution fusion | flops 69992448 | bytes 2765440 | tf_op jit(solution)/shard_map/while/body/eval_jaxpr/fhn,nhd->fhd/dot_general | solution.py:40
  132.3 0.8 copy.26
  (17 shorter events, 0.1 us)
Async XLA Ops:
  0.6 89.7 %copy-start = (bf16[1024,512]{1,0:T(8,128)(2,1)S(1)}, bf16[1024,512]{1,0:T(8,128)(2,1)}, u32[]{:S(2)}) copy-start(bf16[1024,512]{1,0:T(8,128)(2,1)} %param.16) | copy-start | bytes 3145732
  1.9 31.7 %copy-start.1 = (bf16[2,128,512]{1,2,0:T(8,128)(2,1)}, bf16[2,128,512]{1,2,0:T(8,128)(2,1)S(1)}, u32[]{:S(2)}) copy-start(bf16[2,128,512]{1,2,0:T(8,128)(2,1)S(1)} %copy.17) | copy-start | bytes 786436
  2.6 0.5 copy-start.8
  3.3 31.4 %collective-permute-start = (bf16[2,64,512]{1,2,0:T(8,128)(2,1)S(1)}, bf16[2,64,512]{1,2,0:T(8,128)(2,1)S(1)}, u32[]{:S(2)}, u32[]{:S(2)}) collective-permute-start(bf16[2,64,512]{1,2,0:T(8,128)(2,1)S(1)} %get-tuple-element.22), channel_id=1, source_target_pairs={{0,8},{8,16},{16,24},{1,9},{9,17},{17,25},{2,10},{10,18},{18,26},{... | collective-permute-start | bytes 393224 | tf_op jit(solution)/shard_map/ppermute | solution.py:18
  8.3 25.3 %copy-start.10 = (bf16[512]{0:T(512)(128)(2,1)S(1)}, bf16[512]{0:T(512)(128)(2,1)}, u32[]{:S(2)}) copy-start(bf16[512]{0:T(512)(128)(2,1)} %param.12) | copy-start | bytes 3076
  8.3 25.8 %copy-start.11 = (s32[2]{0:T(128)S(1)}, s32[2]{0:T(128)}, u32[]{:S(2)}) copy-start(s32[2]{0:T(128)} %param.10) | copy-start | bytes 28
  8.3 26.5 %collective-permute-start.1 = (bf16[2,64,512]{1,2,0:T(8,128)(2,1)S(1)}, bf16[2,64,512]{1,2,0:T(8,128)(2,1)S(1)}, u32[]{:S(2)}, u32[]{:S(2)}) collective-permute-start(bf16[2,64,512]{1,2,0:T(8,128)(2,1)S(1)} %get-tuple-element.23), channel_id=1, source_target_pairs={{8,0},{16,8},{24,16},{9,1},{17,9},{25,17},{10,2},{18,10},{26,18},{... | collective-permute-start | bytes 393224 | tf_op jit(solution)/shard_map/ppermute | solution.py:19
  37.2 41.8 %copy-start.2 = (bf16[2,128,512]{1,2,0:T(8,128)(2,1)S(1)}, bf16[2,128,512]{1,2,0:T(8,128)(2,1)}, u32[]{:S(2)}) copy-start(bf16[2,128,512]{1,2,0:T(8,128)(2,1)} %copy-done.1) | copy-start | bytes 786436
  37.2 41.8 %copy-start.5 = (f32[512]{0:T(512)S(1)}, f32[512]{0:T(512)}, u32[]{:S(2)}) copy-start(f32[512]{0:T(512)} %convert_element_type.59) | copy-start | bytes 6148
  37.2 41.9 %copy-start.9 = (pred[2,128]{1,0:T(4,128)(4,1)S(1)}, pred[2,128]{1,0:T(4,128)(4,1)}, u32[]{:S(2)}) copy-start(pred[2,128]{1,0:T(4,128)(4,1)} %copy-done.8) | copy-start | bytes 772
  78.3 11.7 %copy-start.6 = (f32[1024]{0:T(1024)S(1)}, f32[1024]{0:T(1024)}, u32[]{:S(2)}) copy-start(f32[1024]{0:T(1024)} %param.14) | copy-start | bytes 12292
  78.3 11.7 %copy-start.7 = (f32[1024]{0:T(1024)S(1)}, f32[1024]{0:T(1024)}, u32[]{:S(2)}) copy-start(f32[1024]{0:T(1024)} %param.13) | copy-start | bytes 12292
  81.0 8.6 %all-to-all-start = ((bf16[2,128,512]{1,2,0:T(8,128)(2,1)}), bf16[2,128,512]{1,2,0:T(8,128)(2,1)S(1)}, u32[]{:S(2)}, u32[]{:S(2)}) async-start(bf16[2,128,512]{1,2,0:T(8,128)(2,1)} %fusion.17), calls=%async_computation | async-start | bytes 524288 | tf_op jit(solution)/shard_map/all_to_all | solution.py:104
  87.5 21.1 %copy-start.3 = (bf16[1024,512]{1,0:T(8,128)(2,1)S(1)}, bf16[1024,512]{1,0:T(8,128)(2,1)}, u32[]{:S(2)}) copy-start(bf16[1024,512]{1,0:T(8,128)(2,1)} %param.15) | copy-start | bytes 3145732
  109.1 2.4 %copy-start.4 = (bf16[1024,512]{1,0:T(8,128)(2,1)S(1)}, bf16[1024,512]{1,0:T(8,128)(2,1)}, u32[]{:S(2)}) copy-start(bf16[1024,512]{1,0:T(8,128)(2,1)} %param.17) | copy-start | bytes 3145732
where the time goes:
time: 134 us; the launch traced here: 133 us
  matrix products  45.6 us (34%)
  local copies, waits for them, and re-layouts  35.1 us (26%)
  blocking collectives  33.5 us (25%)
  starting transfers between devices  9.68 us (7%)
  other arithmetic  6.15 us (5%)
  waiting for transfers between devices  2.11 us (2%)
    conv_general_dilated x1, matrix products, per_device(): lax.conv_general_dilated(padded[:, :frame_rows + kernel_width - 1], kerne...  41.1 us
    unnamed x28, local copies, waits for them, and re-layouts  28.3 us
    all_gather x1, blocking collectives, per_device(): lax.all_gather(key_flat, 'ctx', axis=0, tiled=True)  16.9 us
    all_gather x1, blocking collectives, per_device(): lax.all_gather(val_flat, 'ctx', axis=0, tiled=True)  16.6 us
    ppermute x1, starting transfers between devices, padded_2(): before = lax.ppermute(last, axis, up)  4.94 us
    all_to_all x1, starting transfers between devices, per_device(): lax.all_to_all(hidden, 'fsdp', split_axis=0, concat_axis=2, tiled=True)  3.44 us
  transfers between devices with their start and end apart: 3, of which 1 were waited for; matrix products, arithmetic and copies ran while one was open for 21% of the time, Pallas kernels for 0%

commit v1 on v0

--- a/solution.py
+++ b/solution.py
@@ -115,10 +115,8 @@
     head_count = query_flat.shape[1] // HD
     queries = query_flat.reshape(frame_rows, head_count, HD)
     block_rows = 4 * frame_rows
-    whole_keys, whole_vals = (
-        lax.all_gather(key_flat, "ctx", axis=0, tiled=True),
-        lax.all_gather(val_flat, "ctx", axis=0, tiled=True),
-    )
+    both = lax.all_gather(jnp.concatenate([key_flat, val_flat], axis=1), "ctx", axis=0, tiled=True)
+    whole_keys, whole_vals = both[:, : key_flat.shape[1]], both[:, key_flat.shape[1] :]
     final = blockwise(
         start_state(frame_rows, head_count), whole_keys, whole_vals, queries, own_length, block_rows
     )

time: 134 us -> 143 us (1.067)
  blocking collectives: 33.5 us -> 7.76 us
  waiting for transfers between devices: 2.11 us -> 26.2 us
  between operations: 0.9 us -> 14.3 us
  starting transfers between devices: 9.68 us -> 6.27 us
    all_gather x2 -> x0, blocking collectives: 33.5 us -> none  [the longest x1 16.9 us: per_device(): lax.all_gather(key_flat, 'ctx', axis=0, tiled=True)]
    all_gather x0 -> x1, waiting for transfers between devices: none -> 26.2 us  [per_device(): lax.all_gather(jnp.concatenate([key_flat, val_flat], axis=1), 'ctx', axis...]
    all_to_all x0 -> x1, blocking collectives: none -> 7.76 us  [per_device(): lax.all_to_all(hidden, 'fsdp', split_axis=0, concat_axis=2, tiled=True)]
    slice x0 -> x3, local copies, waits for them, and re-layouts: none -> 5.15 us  [the longest x2 3.1 us: per_device(): both[:, :key_flat.shape[1]]]
    all_to_all x1 -> x0, starting transfers between devices: 3.44 us -> none  [per_device(): lax.all_to_all(hidden, 'fsdp', split_axis=0, concat_axis=2, tiled=True)]
    all_gather x2 -> x0, local copies, waits for them, and re-layouts: 3.05 us -> none  [the longest x1 2.04 us: per_device(): lax.all_gather(val_flat, 'ctx', axis=0, tiled=True)]
    all_to_all x1 -> x0, waiting for transfers between devices: 2.11 us -> none  [per_device(): lax.all_to_all(hidden, 'fsdp', split_axis=0, concat_axis=2, tiled=True)]
  transfers between devices with their start and end apart: 3 -> 3, of which waited for: 1 -> 1; matrix products, arithmetic and copies ran while one was open for 21% -> 19% of each run, Pallas kernels for 0% -> 0%
where the time goes in v1:
time: 143 us
  matrix products  45.5 us (32%)
  local copies, waits for them, and re-layouts  36.2 us (25%)
  waiting for transfers between devices  26.2 us (18%)
  between operations  14.3 us (10%)
  blocking collectives  7.76 us (5%)
  starting transfers between devices  6.27 us (4%)
  other arithmetic  6.24 us (4%)
    conv_general_dilated x1, matrix products, per_device(): lax.conv_general_dilated(padded[:, :frame_rows + kernel_width - 1], kerne...  41.1 us
    unnamed x28, local copies, waits for them, and re-layouts  27.4 us
    all_gather x1, waiting for transfers between devices, per_device(): lax.all_gather(jnp.concatenate([key_flat, val_flat], axis=1), 'ctx', axis...  26.2 us
    all_to_all x1, blocking collectives, per_device(): lax.all_to_all(hidden, 'fsdp', split_axis=0, concat_axis=2, tiled=True)  7.76 us
    ppermute x1, starting transfers between devices, padded_2(): before = lax.ppermute(last, axis, up)  4.94 us
    slice x2, local copies, waits for them, and re-layouts, per_device(): both[:, :key_flat.shape[1]]  3.1 us
  transfers between devices with their start and end apart: 3, of which 1 were waited for; matrix products, arithmetic and copies ran while one was open for 19% of the time, Pallas kernels for 0%

profile of v1, /device:TPU:0, one launch (start us, length us, event | category | flops | bytes accessed | tf_op | source)
XLA Modules:
  0.0 142.5 jit_solution(2669789858870461635)
XLA Ops:
  7.2 0.0 copy-start
  7.2 0.0 all-gather.2.cloned.1.call-start
  7.2 1.2 copy.17
  8.4 0.0 copy-start.1
  8.5 0.8 broadcast_compare_fusion
  9.2 0.5 copy-done.8
  9.8 0.1 fusion.36
  9.9 4.9 %collective-permute-start = (bf16[2,64,512]{1,2,0:T(8,128)(2,1)S(1)}, bf16[2,64,512]{1,2,0:T(8,128)(2,1)S(1)}, u32[]{:S(2)}, u32[]{:S(2)}) collective-permute-start(bf16[2,64,512]{1,2,0:T(8,128)(2,1)S(1)} %get-tuple-element.32), channel_id=1, source_target_pairs={{0,8},{8,16},{16,24},{1,9},{9,17},{17,25},{2,10},{10,18},{18,26},{... | collective-permute-start | bytes 393224 | tf_op jit(solution)/shard_map/ppermute | solution.py:18
  14.8 0.0 copy-start.10
  14.9 1.3 collective-permute-start.1
  16.2 24.0 %copy.19 = bf16[8,128,64,64]{3,2,0,1:T(8,128)(2,1)} copy(bf16[8,128,64,64]{1,3,2,0:T(8,128)(2,1)} %param.11) | data formatting | bytes 16777216 | tf_op args[2]
  40.1 0.0 copy-done.1
  40.1 0.6 convert_element_type.59
  40.7 0.0 collective-permute-done
  40.7 0.0 collective-permute-done.1
  40.7 0.3 pad_maximum_fusion
  41.1 2.1 %copy.18 = bf16[2,255,8,64]{3,0,2,1:T(2,128)(2,1)} copy(bf16[2,255,8,64]{1,3,2,0:T(8,128)(2,1)S(1)} %bitcast.62) | data formatting | bytes 1044480 | tf_op jit(solution)/shard_map/slice | solution.py:92
  43.2 41.1 %fusion.37 = f32[2,128,8,64]{3,0,2,1:T(2,128)S(1)} fusion(bf16[2,255,8,64]{3,0,2,1:T(2,128)(2,1)} %copy.18, bf16[8,128,64,64]{3,2,0,1:T(8,128)(2,1)} %copy.19), kind=kOutput, calls=%fused_computation.68 | convolution fusion | flops 2147483648 | bytes 9435136 | tf_op jit(solution)/shard_map/conv_general_dilated | solution.py:91
  84.2 0.0 copy-start.6
  84.3 0.0 copy-start.7
  84.3 0.7 copy.20
  85.0 0.0 copy-start.3
  85.0 1.3 fusion.17
  86.3 7.8 %all_to_all.4 = bf16[2,128,512]{1,2,0:T(8,128)(2,1)S(1)} all-to-all(bf16[2,128,512]{1,2,0:T(8,128)(2,1)S(1)} %fusion.17), channel_id=1, replica_groups=mesh['ctx'=4,'fsdp'=2,'rep'=4] {'fsdp'}, dimensions={0} | all-to-all | bytes 524288 | tf_op jit(solution)/shard_map/all_to_all | solution.py:104
  94.1 0.2 convert_reduce_fusion
  94.2 0.2 fusion.22
  94.4 0.0 copy-done.7
  94.4 0.0 copy-start.11
  94.4 0.3 fusion.29
  94.8 0.0 copy-start.4
  94.8 0.3 convolution_convert_fusion.1
  95.1 0.3 convolution_convert_fusion.2
  95.5 0.7 pad_maximum_fusion.2
  96.2 0.0 all-gather.2.cloned.1.call-update
  96.3 0.6 dynamic_slice.11
  96.8 0.6 iota_compare_fusion
  97.5 0.7 broadcast_compare_fusion.1
  98.2 0.9 copy.25
  99.0 0.3 convolution_convert_fusion
  99.4 0.1 copy.22
  99.5 26.2 %all-gather.2.cloned.1.call-done = bf16[512,1024]{1,0:T(8,128)(2,1)} async-done(((bf16[128,1024]{1,0:T(8,128)(2,1)}), bf16[512,1024]{1,0:T(8,128)(2,1)}) %all-gather.2.cloned.1.call-update) | async-done | bytes 1048592 | tf_op jit(solution)/shard_map/all_gather | solution.py:118
  125.7 2.1 %fusion.35 = (bf16[512,512]{1,0:T(8,128)(2,1)S(1)}, bf16[512,512]{1,0:T(8,128)(2,1)}) fusion(bf16[512,1024]{1,0:T(8,128)(2,1)} %all-gather.2.cloned.1.call-done), kind=kLoop, calls=%fused_computation.66 | loop fusion | bytes 2097152 | tf_op jit(solution)/shard_map/slice | solution.py:119
  127.8 1.0 copy.21
  128.8 1.7 %bitcast_reduce_fusion = (f32[128,8]{0,1:T(8,128)S(1)}, f32[8,512,128]{2,1,0:T(8,128)S(1)}) fusion(pred[512]{0:T(512)(128)(4,1)S(1)} %iota_compare_fusion, bf16[512,8,64]{0,2,1:T(8,128)(2,1)} %bitcast.63, bf16[128,8,64]{0,2,1:T(8,128)(2,1)S(1)} %bitcast.64), kind=kOutput, calls=%fused_computation.1 | convolution fusion | flops 68680704 | bytes 2757120 | tf_op jit(solution)/shard_map/while/body/eval_jaxpr/fhd,nhd->fhn/dot_general | solution.py:31
  130.5 0.6 fusion.2
  131.1 2.1 %copy.23 = bf16[512,512]{0,1:T(8,128)(2,1)} copy(bf16[512,512]{1,0:T(8,128)(2,1)} %get-tuple-element.23) | data formatting | bytes 1048576 | tf_op jit(solution)/shard_map/slice | solution.py:119
  133.1 1.8 %fusion.7 = bf16[128,8,64]{0,2,1:T(8,128)(2,1)S(1)} fusion(bf16[512,8,64]{0,2,1:T(8,128)(2,1)} %bitcast.65, f32[8,512,128]{2,1,0:T(8,128)S(1)} %get-tuple-element.37, f32[128,8]{0,1:T(8,128)S(1)} %broadcast_maximum_fusion, pred[512]{0:T(512)(128)(4,1)S(1)} %iota_compare_fusion, f32[128,8]{0,1:T(8,128)S(1)} %get-tuple-element.35, ...), kind=kOutput, calls=%fused_computation.11 | convolution fusion | flops 69992448 | bytes 2765440 | tf_op jit(solution)/shard_map/while/body/eval_jaxpr/fhn,nhd->fhd/dot_general | solution.py:40
  134.9 0.8 copy.26
  (19 shorter events, 0.1 us)
Async XLA Ops:
  7.2 87.6 %copy-start = (bf16[1024,512]{1,0:T(8,128)(2,1)S(1)}, bf16[1024,512]{1,0:T(8,128)(2,1)}, u32[]{:S(2)}) copy-start(bf16[1024,512]{1,0:T(8,128)(2,1)} %param.17) | copy-start | bytes 3145732
  7.2 118.5 %all-gather.2.cloned.1.call-start = ((), (), s32[]{:S(2)}) async-start(), calls=%async_computation.1 | async-start | bytes 1310720 | tf_op jit(solution)/shard_map/all_gather | solution.py:118
  8.4 31.7 %copy-start.1 = (bf16[2,128,512]{1,2,0:T(8,128)(2,1)}, bf16[2,128,512]{1,2,0:T(8,128)(2,1)S(1)}, u32[]{:S(2)}) copy-start(bf16[2,128,512]{1,2,0:T(8,128)(2,1)S(1)} %copy.17) | copy-start | bytes 786436
  9.2 0.5 copy-start.8
  9.9 30.8 %collective-permute-start = (bf16[2,64,512]{1,2,0:T(8,128)(2,1)S(1)}, bf16[2,64,512]{1,2,0:T(8,128)(2,1)S(1)}, u32[]{:S(2)}, u32[]{:S(2)}) collective-permute-start(bf16[2,64,512]{1,2,0:T(8,128)(2,1)S(1)} %get-tuple-element.32), channel_id=1, source_target_pairs={{0,8},{8,16},{16,24},{1,9},{9,17},{17,25},{2,10},{10,18},{18,26},{... | collective-permute-start | bytes 393224 | tf_op jit(solution)/shard_map/ppermute | solution.py:18
  14.8 25.3 %copy-start.10 = (bf16[512]{0:T(512)(128)(2,1)S(1)}, bf16[512]{0:T(512)(128)(2,1)}, u32[]{:S(2)}) copy-start(bf16[512]{0:T(512)(128)(2,1)} %param.12) | copy-start | bytes 3076
  14.9 25.9 %collective-permute-start.1 = (bf16[2,64,512]{1,2,0:T(8,128)(2,1)S(1)}, bf16[2,64,512]{1,2,0:T(8,128)(2,1)S(1)}, u32[]{:S(2)}, u32[]{:S(2)}) collective-permute-start(bf16[2,64,512]{1,2,0:T(8,128)(2,1)S(1)} %get-tuple-element.33), channel_id=1, source_target_pairs={{8,0},{16,8},{24,16},{9,1},{17,9},{25,17},{10,2},{18,10},{26,18},{... | collective-permute-start | bytes 393224 | tf_op jit(solution)/shard_map/ppermute | solution.py:19
  43.2 41.8 %copy-start.2 = (bf16[2,128,512]{1,2,0:T(8,128)(2,1)S(1)}, bf16[2,128,512]{1,2,0:T(8,128)(2,1)}, u32[]{:S(2)}) copy-start(bf16[2,128,512]{1,2,0:T(8,128)(2,1)} %copy-done.1) | copy-start | bytes 786436
  43.2 41.8 %copy-start.5 = (f32[512]{0:T(512)S(1)}, f32[512]{0:T(512)}, u32[]{:S(2)}) copy-start(f32[512]{0:T(512)} %convert_element_type.59) | copy-start | bytes 6148
  43.2 41.9 %copy-start.9 = (pred[2,128]{1,0:T(4,128)(4,1)S(1)}, pred[2,128]{1,0:T(4,128)(4,1)}, u32[]{:S(2)}) copy-start(pred[2,128]{1,0:T(4,128)(4,1)} %copy-done.8) | copy-start | bytes 772
  84.2 10.1 %copy-start.6 = (f32[1024]{0:T(1024)S(1)}, f32[1024]{0:T(1024)}, u32[]{:S(2)}) copy-start(f32[1024]{0:T(1024)} %param.14) | copy-start | bytes 12292
  84.3 10.1 %copy-start.7 = (f32[1024]{0:T(1024)S(1)}, f32[1024]{0:T(1024)}, u32[]{:S(2)}) copy-start(f32[1024]{0:T(1024)} %param.13) | copy-start | bytes 12292
  85.0 10.1 %copy-start.3 = (bf16[1024,512]{1,0:T(8,128)(2,1)S(1)}, bf16[1024,512]{1,0:T(8,128)(2,1)}, u32[]{:S(2)}) copy-start(bf16[1024,512]{1,0:T(8,128)(2,1)} %param.16) | copy-start | bytes 3145732
  94.4 1.9 %copy-start.11 = (s32[2]{0:T(128)S(1)}, s32[2]{0:T(128)}, u32[]{:S(2)}) copy-start(s32[2]{0:T(128)} %param.10) | copy-start | bytes 28
  94.8 4.3 %copy-start.4 = (bf16[1024,512]{1,0:T(8,128)(2,1)S(1)}, bf16[1024,512]{1,0:T(8,128)(2,1)}, u32[]{:S(2)}) copy-start(bf16[1024,512]{1,0:T(8,128)(2,1)} %param.15) | copy-start | bytes 3145732
Sparse Core Ops, SparseCore 0:
  96.4 29.2 all-gather.1

commit v2 on v0

--- a/solution.py
+++ b/solution.py
@@ -4,6 +4,8 @@
 import jax.numpy as jnp
 from jax import lax
 from jax.sharding import PartitionSpec as P
+from jax.experimental import pallas as pl
+from jax.experimental.pallas import tpu as pltpu
 
 HD = 64
 
@@ -19,6 +21,45 @@
         after = lax.ppermute(first, axis, down)
         x = jnp.concatenate([before, x, after], axis=dim)
     return x
+
+
+TAP_STEP = 16
+
+
+def conv_body(x_ref, w_ref, out_ref):
+    recs, rows, width = x_ref.shape[1], out_ref.shape[2], x_ref.shape[3]
+    taps = w_ref.shape[1]
+    acc = jnp.zeros((recs * rows, w_ref.shape[3]), jnp.float32)
+    for chunk in range(taps // TAP_STEP):
+        lhs = x_ref[0, :, chunk * TAP_STEP : chunk * TAP_STEP + rows, :].reshape(recs * rows, width)
+        rhs = w_ref[0, chunk * TAP_STEP : (chunk + 1) * TAP_STEP].reshape(width, w_ref.shape[3])
+        acc = acc + jnp.dot(lhs, rhs, preferred_element_type=jnp.float32)
+    out_ref[0] = acc.reshape(recs, rows, w_ref.shape[3])
+
+
+def grouped_conv(padded, conv_weight, frame_rows):
+    recs = padded.shape[0]
+    groups_here, taps, group_in, group_out = conv_weight.shape
+    span = frame_rows + taps - TAP_STEP
+    grouped = padded.reshape(recs, padded.shape[1], groups_here, group_in)
+    shifted = jnp.stack([grouped[:, j : j + span] for j in range(TAP_STEP)], axis=3)
+    expanded = shifted.transpose(2, 0, 1, 3, 4).reshape(groups_here, recs, span, TAP_STEP * group_in)
+    out = pl.pallas_call(
+        conv_body,
+        grid=(groups_here,),
+        in_specs=[
+            pl.BlockSpec((1, recs, span, TAP_STEP * group_in), lambda g: (g, 0, 0, 0)),
+            pl.BlockSpec((1, taps, group_in, group_out), lambda g: (g, 0, 0, 0)),
+        ],
+        out_specs=pl.BlockSpec((1, recs, frame_rows, group_out), lambda g: (g, 0, 0, 0)),
+        out_shape=jax.ShapeDtypeStruct((groups_here, recs, frame_rows, group_out), jnp.float32),
+        cost_estimate=pl.CostEstimate(
+            flops=2 * groups_here * recs * frame_rows * taps * group_in * group_out,
+            bytes_accessed=expanded.size * 2 + conv_weight.size * 2 + groups_here * recs * frame_rows * group_out * 4,
+            transcendentals=0,
+        ),
+    )(expanded, conv_weight)
+    return out.transpose(1, 2, 0, 3).reshape(recs, frame_rows, groups_here * group_out)
 
 
 def attend(carry, piece, start, queries, own_length):
@@ -85,18 +126,7 @@
     groups_here, kernel_width, group_in, group_out = conv_weight.shape
     half_width = kernel_width // 2
     padded = padded_2(masked, (("ctx", 1),), half_width)
-    kernel = conv_weight.transpose(1, 2, 0, 3).reshape(
-        kernel_width, group_in, groups_here * group_out
-    )
-    conv_out = lax.conv_general_dilated(
-        padded[:, : frame_rows + kernel_width - 1],
-        kernel,
-        (1,),
-        "VALID",
-        dimension_numbers=("NWC", "WIO", "NWC"),
-        feature_group_count=groups_here,
-        preferred_element_type=jnp.float32,
-    )
+    conv_out = grouped_conv(padded, conv_weight, frame_rows)
     hidden = (
         masked.astype(jnp.float32)
         + jax.nn.gelu(conv_out + conv_bias.astype(jnp.float32), approximate=False)

time: 134 us -> 126 us (0.940)
  matrix products: 45.6 us -> 5.66 us
  local copies, waits for them, and re-layouts: 35.1 us -> 51.6 us
  Pallas kernels: 0 us -> 15.1 us
    conv_general_dilated x1 -> x0, matrix products: 41.1 us -> none  [per_device(): lax.conv_general_dilated(padded[:, :frame_rows + kernel_width - 1], kerne...]
    pallas_call x0 -> x1, Pallas kernels: none -> 15.1 us  [grouped_conv(): pl.pallas_call(conv_body, grid=(groups_here,), in_specs=[pl.BlockSpec((1,...]
    reshape x0 -> x1, local copies, waits for them, and re-layouts: none -> 11.4 us  [grouped_conv(): shifted.transpose(2, 0, 1, 3, 4)]
    unnamed x28 -> x33, local copies, waits for them, and re-layouts: 28.3 us -> 34.5 us
    slice x1 -> x0, local copies, waits for them, and re-layouts: 2.1 us -> none  [per_device(): padded[:, :frame_rows + kernel_width - 1]]
    transpose x0 -> x1, local copies, waits for them, and re-layouts: none -> 1.54 us  [grouped_conv(): out.transpose(1, 2, 0, 3).reshape(recs, frame_rows, groups_here * group_out)]
  transfers between devices with their start and end apart: 3 -> 3, of which waited for: 1 -> 1; matrix products, arithmetic and copies ran while one was open for 21% -> 22% of each run, Pallas kernels for 0% -> 0%
where the time goes in v2:
time: 126 us; the launch traced here: 124 us
  local copies, waits for them, and re-layouts  51.6 us (41%)
  blocking collectives  33.7 us (27%)
  Pallas kernels  15.1 us (12%)
  starting transfers between devices  9.68 us (8%)
  matrix products  5.66 us (4%)
  other arithmetic  5.6 us (4%)
  waiting for transfers between devices  2.05 us (2%)
    unnamed x33, local copies, waits for them, and re-layouts  34.5 us
    all_gather x1, blocking collectives, per_device(): lax.all_gather(key_flat, 'ctx', axis=0, tiled=True)  17.1 us
    all_gather x1, blocking collectives, per_device(): lax.all_gather(val_flat, 'ctx', axis=0, tiled=True)  16.6 us
    pallas_call x1, Pallas kernels, grouped_conv(): pl.pallas_call(conv_body, grid=(groups_here,), in_specs=[pl.BlockSpec((1,...  15.1 us
    reshape x1, local copies, waits for them, and re-layouts, grouped_conv(): shifted.transpose(2, 0, 1, 3, 4)  11.4 us
    ppermute x1, starting transfers between devices, padded_2(): before = lax.ppermute(last, axis, up)  4.94 us
    all_to_all x1, starting transfers between devices, per_device(): lax.all_to_all(hidden, 'fsdp', split_axis=0, concat_axis=2, tiled=True)  3.44 us
  transfers between devices with their start and end apart: 3, of which 1 were waited for; matrix products, arithmetic and copies ran while one was open for 22% of the time, Pallas kernels for 0%

profile of v2, /device:TPU:0, one launch (start us, length us, event | category | flops | bytes accessed | tf_op | source)
XLA Modules:
  0.0 124.4 jit_solution(7278879226522258379)
XLA Ops:
  0.7 1.2 copy.33
  1.9 0.7 broadcast_compare_fusion
  2.6 0.1 fusion.51
  2.8 4.9 %collective-permute-start = (bf16[2,64,512]{1,2,0:T(8,128)(2,1)S(1)}, bf16[2,64,512]{1,2,0:T(8,128)(2,1)S(1)}, u32[]{:S(2)}, u32[]{:S(2)}) collective-permute-start(bf16[2,64,512]{1,2,0:T(8,128)(2,1)S(1)} %get-tuple-element.22), channel_id=1, source_target_pairs={{0,8},{8,16},{16,24},{1,9},{9,17},{17,25},{2,10},{10,18},{18,26},{... | collective-permute-start | bytes 393224 | tf_op jit(solution)/shard_map/ppermute | solution.py:20
  7.7 1.3 %collective-permute-start.1 = (bf16[2,64,512]{1,2,0:T(8,128)(2,1)S(1)}, bf16[2,64,512]{1,2,0:T(8,128)(2,1)S(1)}, u32[]{:S(2)}, u32[]{:S(2)}) collective-permute-start(bf16[2,64,512]{1,2,0:T(8,128)(2,1)S(1)} %get-tuple-element.23), channel_id=1, source_target_pairs={{8,0},{16,8},{24,16},{9,1},{17,9},{25,17},{10,2},{18,10},{26,18},{... | collective-permute-start | bytes 393224 | tf_op jit(solution)/shard_map/ppermute | solution.py:21
  9.0 23.9 %copy.36.w_ref = bf16[8,128,64,64]{3,2,1,0:T(8,128)(2,1)} copy(bf16[8,128,64,64]{1,3,2,0:T(8,128)(2,1)} %param.11) | data formatting | bytes 16777216 | tf_op args[2]
  33.0 0.6 dynamic_slice.11
  33.6 0.3 pad_maximum_fusion
  34.0 0.2 fusion.32
  34.2 0.2 fusion.31
  34.5 0.2 fusion.30
  34.7 0.2 fusion.29
  35.0 0.2 fusion.28
  35.3 0.2 fusion.27
  35.5 0.2 fusion.26
  35.8 0.2 fusion.25
  36.0 0.2 fusion.24
  36.3 0.2 fusion.23
  36.5 0.2 fusion.22
  36.8 0.2 fusion.21
  37.1 0.2 fusion.20
  37.3 0.2 fusion.19
  37.6 0.2 fusion.18
  37.8 3.2 %copy-done.1 = bf16[2,240,8,16,64]{1,4,3,2,0:T(8,128)(2,1)} copy-done((bf16[2,240,8,16,64]{1,4,3,2,0:T(8,128)(2,1)}, bf16[2,240,8,16,64]{1,4,3,2,0:T(8,128)(2,1)S(1)}, u32[]{:S(2)}) %copy-start.1) | copy-done | bytes 7864344
  41.0 11.4 %copy.35.x_ref = bf16[8,2,240,1024]{3,2,1,0:T(8,128)(2,1)} copy(bf16[8,2,240,1024]{2,3,0,1:T(8,128)(2,1)} %bitcast.144) | data formatting | bytes 15728640 | tf_op jit(solution)/shard_map/reshape | solution.py:46
  52.5 15.1 %shard_map.104 = f32[8,2,128,64]{3,2,1,0:T(8,128)} custom-call(bf16[8,2,240,1024]{3,2,1,0:T(8,128)(2,1)} %copy.35.x_ref, bf16[8,128,64,64]{3,2,1,0:T(8,128)(2,1)} %copy.36.w_ref), custom_call_target="tpu_custom_call" | custom-call | flops 2147483648 | bytes 16777216 | tf_op jit(solution)/shard_map/pallas_call | solution.py:47
  67.6 1.5 %copy.37 = f32[2,128,8,64]{1,3,2,0:T(8,128)S(1)} copy(f32[2,128,8,64]{3,1,0,2:T(8,128)} %bitcast.145) | data formatting | bytes 1048576 | tf_op jit(solution)/shard_map/transpose | solution.py:62
  69.2 2.0 %fusion.17 = bf16[2,128,512]{1,2,0:T(8,128)(2,1)} fusion(f32[2,128,8,64]{1,3,2,0:T(8,128)S(1)} %copy.37, f32[512]{0:T(512)S(1)} %convert_element_type.59, bf16[2,128,512]{1,2,0:T(8,128)(2,1)S(1)} %copy.33, pred[2,128]{1,0:T(4,128)(4,1)S(1)} %broadcast_compare_fusion), kind=kLoop, calls=%fused_computation.24 | loop fusion | flops 9043968 | bytes 1050880 | tf_op jit(solution)/shard_map/convert_element_type | solution.py:133
  71.1 3.4 %all-to-all-start = ((bf16[2,128,512]{1,2,0:T(8,128)(2,1)}), bf16[2,128,512]{1,2,0:T(8,128)(2,1)S(1)}, u32[]{:S(2)}, u32[]{:S(2)}) async-start(bf16[2,128,512]{1,2,0:T(8,128)(2,1)} %fusion.17), calls=%async_computation | async-start | bytes 524288 | tf_op jit(solution)/shard_map/all_to_all | solution.py:134
  74.6 0.7 iota_compare_fusion
  75.2 0.7 broadcast_compare_fusion.1
  75.9 1.8 %copy.42 = bf16[2,128,512]{2,1,0:T(8,128)(2,1)} copy(bf16[2,128,512]{1,2,0:T(8,128)(2,1)} %fusion.17) | data formatting | bytes 524288
  77.7 2.0 %all-to-all-done = bf16[2,128,512]{1,2,0:T(8,128)(2,1)S(1)} async-done(((bf16[2,128,512]{1,2,0:T(8,128)(2,1)}), bf16[2,128,512]{1,2,0:T(8,128)(2,1)S(1)}, u32[]{:S(2)}, u32[]{:S(2)}) %all-to-all-start) | async-done | bytes 262176 | tf_op jit(solution)/shard_map/all_to_all | solution.py:134
  79.7 0.2 convert_reduce_fusion
  79.9 0.2 fusion.38
  80.1 0.3 fusion.45
  80.4 0.3 convolution_convert_fusion.2
  80.8 17.1 %all_gather.6 = bf16[512,512]{1,0:T(8,128)(2,1)S(1)} all-gather(bf16[128,512]{1,0:T(8,128)(2,1)S(1)} %convolution_convert_fusion.2), channel_id=1, replica_groups=mesh['ctx'=4,'fsdp'=2,'rep'=4] {'ctx'}, dimensions={0}, use_global_device_ids=true | all-gather | bytes 655360 | tf_op jit(solution)/shard_map/all_gather | solution.py:149
  97.9 1.0 copy.38
  98.9 0.3 convolution_convert_fusion.1
  99.2 0.1 copy.39
  99.3 1.7 %bitcast_reduce_fusion = (f32[128,8]{0,1:T(8,128)S(1)}, f32[8,512,128]{2,1,0:T(8,128)S(1)}) fusion(pred[512]{0:T(512)(128)(4,1)S(1)} %iota_compare_fusion, bf16[512,8,64]{0,2,1:T(8,128)(2,1)} %bitcast.146, bf16[128,8,64]{0,2,1:T(8,128)(2,1)S(1)} %bitcast.147), kind=kOutput, calls=%fused_computation.1 | convolution fusion | flops 68680704 | bytes 2757120 | tf_op jit(solution)/shard_map/while/body/eval_jaxpr/fhd,nhd->fhn/dot_general | solution.py:72
  101.0 0.6 fusion.2
  101.6 1.6 %convolution_convert_fusion = bf16[128,512]{1,0:T(8,128)(2,1)S(1)} fusion(bf16[128,1024]{0,1:T(8,128)(2,1)S(1)} %fusion.45, bf16[1024,512]{1,0:T(8,128)(2,1)} %param.17), kind=kOutput, calls=%fused_computation.12 | convolution fusion | flops 134283264 | bytes 1441792 | tf_op jit(solution)/shard_map/dot_general | solution.py:144
  103.2 16.6 %all_gather.7 = bf16[512,512]{1,0:T(8,128)(2,1)} all-gather(bf16[128,512]{1,0:T(8,128)(2,1)S(1)} %convolution_convert_fusion), channel_id=1, replica_groups=mesh['ctx'=4,'fsdp'=2,'rep'=4] {'ctx'}, dimensions={0}, use_global_device_ids=true | all-gather | bytes 655360 | tf_op jit(solution)/shard_map/all_gather | solution.py:150
  119.8 2.0 %copy.40 = bf16[512,512]{0,1:T(8,128)(2,1)} copy(bf16[512,512]{1,0:T(8,128)(2,1)} %all_gather.7) | data formatting | bytes 1048576 | tf_op jit(solution)/shard_map/all_gather | solution.py:150
  121.9 1.8 %fusion.7 = bf16[128,8,64]{0,2,1:T(8,128)(2,1)S(1)} fusion(bf16[512,8,64]{0,2,1:T(8,128)(2,1)} %bitcast.148, f32[8,512,128]{2,1,0:T(8,128)S(1)} %get-tuple-element.35, f32[128,8]{0,1:T(8,128)S(1)} %broadcast_maximum_fusion, pred[512]{0:T(512)(128)(4,1)S(1)} %iota_compare_fusion, f32[128,8]{0,1:T(8,128)S(1)} %get-tuple-element.33, ...), kind=kOutput, calls=%fused_computation.11 | convolution fusion | flops 69992448 | bytes 2765440 | tf_op jit(solution)/shard_map/while/body/eval_jaxpr/fhn,nhd->fhd/dot_general | solution.py:81
  123.6 0.8 copy.43
  (23 shorter events, 0.1 us)
Async XLA Ops:
  0.6 79.8 %copy-start = (bf16[1024,512]{1,0:T(8,128)(2,1)S(1)}, bf16[1024,512]{1,0:T(8,128)(2,1)}, u32[]{:S(2)}) copy-start(bf16[1024,512]{1,0:T(8,128)(2,1)} %param.16) | copy-start | bytes 3145732
  2.8 30.8 %collective-permute-start = (bf16[2,64,512]{1,2,0:T(8,128)(2,1)S(1)}, bf16[2,64,512]{1,2,0:T(8,128)(2,1)S(1)}, u32[]{:S(2)}, u32[]{:S(2)}) collective-permute-start(bf16[2,64,512]{1,2,0:T(8,128)(2,1)S(1)} %get-tuple-element.22), channel_id=1, source_target_pairs={{0,8},{8,16},{16,24},{1,9},{9,17},{17,25},{2,10},{10,18},{18,26},{... | collective-permute-start | bytes 393224 | tf_op jit(solution)/shard_map/ppermute | solution.py:20
  7.7 25.3 %copy-start.5 = (bf16[512]{0:T(512)(128)(2,1)S(1)}, bf16[512]{0:T(512)(128)(2,1)}, u32[]{:S(2)}) copy-start(bf16[512]{0:T(512)(128)(2,1)} %param.12) | copy-start | bytes 3076
  7.7 25.3 %copy-start.6 = (s32[2]{0:T(128)S(1)}, s32[2]{0:T(128)}, u32[]{:S(2)}) copy-start(s32[2]{0:T(128)} %param.10) | copy-start | bytes 28
  7.7 25.8 %collective-permute-start.1 = (bf16[2,64,512]{1,2,0:T(8,128)(2,1)S(1)}, bf16[2,64,512]{1,2,0:T(8,128)(2,1)S(1)}, u32[]{:S(2)}, u32[]{:S(2)}) collective-permute-start(bf16[2,64,512]{1,2,0:T(8,128)(2,1)S(1)} %get-tuple-element.23), channel_id=1, source_target_pairs={{8,0},{16,8},{24,16},{9,1},{17,9},{25,17},{10,2},{18,10},{26,18},{... | collective-permute-start | bytes 393224 | tf_op jit(solution)/shard_map/ppermute | solution.py:21
  37.8 3.2 %copy-start.1 = (bf16[2,240,8,16,64]{1,4,3,2,0:T(8,128)(2,1)}, bf16[2,240,8,16,64]{1,4,3,2,0:T(8,128)(2,1)S(1)}, u32[]{:S(2)}) copy-start(bf16[2,240,8,16,64]{1,4,3,2,0:T(8,128)(2,1)S(1)} %fusion.18) | copy-start | bytes 23592964
  52.5 27.6 %copy-start.3 = (f32[1024]{0:T(1024)S(1)}, f32[1024]{0:T(1024)}, u32[]{:S(2)}) copy-start(f32[1024]{0:T(1024)} %param.14) | copy-start | bytes 12292
  52.5 27.6 %copy-start.4 = (f32[1024]{0:T(1024)S(1)}, f32[1024]{0:T(1024)}, u32[]{:S(2)}) copy-start(f32[1024]{0:T(1024)} %param.13) | copy-start | bytes 12292
  52.5 46.4 %copy-start.2 = (bf16[1024,512]{1,0:T(8,128)(2,1)S(1)}, bf16[1024,512]{1,0:T(8,128)(2,1)}, u32[]{:S(2)}) copy-start(bf16[1024,512]{1,0:T(8,128)(2,1)} %param.15) | copy-start | bytes 3145732
  71.1 8.6 %all-to-all-start = ((bf16[2,128,512]{1,2,0:T(8,128)(2,1)}), bf16[2,128,512]{1,2,0:T(8,128)(2,1)S(1)}, u32[]{:S(2)}, u32[]{:S(2)}) async-start(bf16[2,128,512]{1,2,0:T(8,128)(2,1)} %fusion.17), calls=%async_computation | async-start | bytes 524288 | tf_op jit(solution)/shard_map/all_to_all | solution.py:134
